TPU v7x, 128 devices: a whole 4x4x4 slice. The times are simulated.
128 devices in a mesh: cfg: 2 (over core), row: 4 (over z), col: 16 (over y, x).
Axes of the slice: x: 4, y: 4, z: 4, core: 2. Of those that a mesh axis runs over, the one named last changes fastest.
Arguments:
- img_tokens: bfloat16 [2, 16, 1024, 3072], P('cfg', 'col', None, 'row'), may hold values from -6 to 6
- txt_tokens: bfloat16 [2, 16, 512, 3072], P('cfg', 'col', None, 'row'), may hold values from -6 to 6
- img_mod: bfloat16 [2, 16, 2, 3072], P('cfg', 'col', None, 'row'), may hold values from -3 to 3
- txt_mod: bfloat16 [2, 16, 2, 3072], P('cfg', 'col', None, 'row'), may hold values from -3 to 3
- img_gate: bfloat16 [2, 16, 3072], P('cfg', 'col', 'row'), may hold values from -16 to 16
- txt_len: int32 [2, 16], P('cfg', 'col'), may hold values from 128 to 512, as said below
- img_qkv_weight: bfloat16 [3072, 3, 3072], P('col', None, 'row'), may hold values from -0.109375 to 0.109375
- txt_kv_weight: bfloat16 [3072, 2, 3072], P('col', None, 'row'), may hold values from -0.109375 to 0.109375
- out_weight: bfloat16 [3072, 3072], P('row', 'col'), may hold values from -0.109375 to 0.109375
- final_weight: bfloat16 [3072, 64], P('row'), may hold values from -0.109375 to 0.109375
- latent: float32 [16, 1024, 64], P('col', ('cfg', 'row')), may hold values from -6 to 6
- sigmas: float32 [5], replicated, may hold values from 0 to 2, as said below
- step_index: int32 [1], replicated, may hold values from 0 to 3
- guidance: float32 [1], replicated, may hold values from 1.5 to 5
Outputs:
- img_out: bfloat16 [2, 16, 1024, 3072], P('cfg', 'col', None, 'row')
- latent_next: float32 [16, 1024, 64], P('col', ('cfg', 'row'))
Inputs may be any that keep to these rules, and one draw needn't show every extreme that they name: `txt_len`: in each half some prompt has all 512 text slots live and some other prompt exactly 128. `sigmas`: falls strictly along the table.
All inputs are finite; a program needn't handle non-finite values.
Results may differ from a plain program's by a relative error of at most 0.015.
Values may be sent and summed in bfloat16 or wider, within the bound.
No kernel may reach another device: no remote copies, remote signals or barrier semaphores. Data moves between devices by JAX's collectives and lax.ppermute only.
A program may use at most 128 MiB of HBM per device.

v0:
```python
import math

import jax
import jax.numpy as jnp
from jax import lax
from jax.sharding import PartitionSpec as P

HD = 128


def modulate(tokens, shift_scale):
    values = tokens.astype(jnp.float32)
    centre = values - jnp.mean(values, -1, keepdims=True)
    spread = jnp.mean(centre * centre, -1, keepdims=True)
    normed = centre * lax.rsqrt(spread + 1e-06)
    scaled = normed * (1.0 + shift_scale[..., 1:2, :].astype(jnp.float32))
    return (scaled + shift_scale[..., 0:1, :].astype(jnp.float32)).astype(jnp.bfloat16)


def rms_norm(values):
    return values * lax.rsqrt(jnp.mean(values * values, -1, keepdims=True) + 1e-06)


def add_rows(piece, ready):
    return jnp.dot(ready, piece.reshape(piece.shape[0], -1), preferred_element_type=jnp.float32)


def shards(
    img_tokens,
    txt_tokens,
    img_mod,
    txt_mod,
    img_gate,
    txt_len,
    img_qkv_weight,
    txt_kv_weight,
    out_weight,
    final_weight,
    latent,
    sigmas,
    step_index,
    guidance,
):
    img_whole, txt_whole, img_shift, txt_shift = (
        lax.all_gather(img_tokens, "row", axis=3, tiled=True),
        lax.all_gather(txt_tokens, "row", axis=3, tiled=True),
        lax.all_gather(img_mod, "row", axis=3, tiled=True),
        lax.all_gather(txt_mod, "row", axis=3, tiled=True),
    )
    prompts = img_tokens.shape[1]
    images = img_tokens.shape[2]
    text_slots = txt_tokens.shape[2]
    local_width = img_qkv_weight.shape[2]
    heads_here = local_width // HD
    img_ready = modulate(img_whole[0], img_shift[0]).reshape(prompts * images, -1)
    txt_ready = modulate(txt_whole[0], txt_shift[0]).reshape(prompts * text_slots, -1)
    img_proj = add_rows(lax.all_gather(img_qkv_weight, "col", axis=0, tiled=True), img_ready)
    txt_proj = add_rows(lax.all_gather(txt_kv_weight, "col", axis=0, tiled=True), txt_ready)
    img_proj = img_proj.reshape(prompts, images, 3, heads_here, HD)
    txt_proj = txt_proj.reshape(prompts, text_slots, 2, heads_here, HD)
    queries = rms_norm(img_proj[:, :, 0]).astype(jnp.bfloat16)
    key_rows = jnp.concatenate(
        [rms_norm(txt_proj[:, :, 0]), rms_norm(img_proj[:, :, 1])], 1
    ).astype(jnp.bfloat16)
    value_rows = jnp.concatenate([txt_proj[:, :, 1], img_proj[:, :, 2]], 1).astype(jnp.bfloat16)
    positions = jnp.arange(text_slots + images, dtype=jnp.int32)
    scores = jnp.einsum(
        "qhe,khe->hqk", queries[0], key_rows[0], preferred_element_type=jnp.float32
    ) / math.sqrt(HD)
    usable = (positions < txt_len[0, 0]) | (positions >= text_slots)
    weights = jnp.where(usable, jnp.exp(scores), 0.0)
    chances = (weights / jnp.sum(weights, -1, keepdims=True)).astype(jnp.bfloat16)
    mixed = jnp.einsum("hqk,khe->qhe", chances, value_rows[0], preferred_element_type=jnp.float32)
    outputs = mixed.reshape(images, local_width).astype(jnp.bfloat16)
    head_terms = jnp.dot(
        outputs,
        lax.all_gather(out_weight, "col", axis=1, tiled=True),
        preferred_element_type=jnp.float32,
    )
    projected = (
        lax.psum_scatter(head_terms.astype(jnp.bfloat16), "row", scatter_dimension=1, tiled=True)
        .astype(jnp.float32)
        .reshape(prompts, images, local_width)
    )
    gating = img_gate[0][:, None, :].astype(jnp.float32)
    img_out = (img_tokens[0].astype(jnp.float32) + gating * projected).astype(jnp.bfloat16)
    velocity = jnp.dot(
        img_out.reshape(prompts * images, local_width),
        final_weight,
        preferred_element_type=jnp.float32,
    )
    velocity = velocity.reshape(prompts, images, -1)
    strength = guidance[0]
    share = jnp.where(lax.axis_index("cfg") == 1, strength, 1.0 - strength)
    weighted = velocity * share
    halved = lax.psum_scatter(weighted.astype(jnp.bfloat16), "cfg", scatter_dimension=1, tiled=True)
    guided = lax.psum_scatter(halved, "row", scatter_dimension=1, tiled=True).astype(jnp.float32)
    position_now = step_index[0]
    step_size = sigmas[position_now + 1] - sigmas[position_now]
    return (img_out[None], latent + step_size * guided)


def solution(mesh):
    return jax.shard_map(
        shards,
        mesh=mesh,
        in_specs=(
            P("cfg", "col", None, "row"),
            P("cfg", "col", None, "row"),
            P("cfg", "col", None, "row"),
            P("cfg", "col", None, "row"),
            P("cfg", "col", "row"),
            P("cfg", "col"),
            P("col", None, "row"),
            P("col", None, "row"),
            P("row", "col"),
            P("row", None),
            P("col", ("cfg", "row"), None),
            P(),
            P(),
            P(),
        ),
        out_specs=(P("cfg", "col", None, "row"), P("col", ("cfg", "row"), None)),
        check_vma=False,
    )
```

profile of v0, /device:TPU:1, one launch (start us, length us, event | category | flops | bytes accessed | tf_op | source)
XLA Modules:
  0.0 492.6 jit_solution(1742859976843953743)
XLA Ops:
  7.2 0.7 all-gather.6.cloned.1.call-update
  8.0 0.7 all-gather.10.cloned.1.call-update
  10.6 11.2 %all_gather.25 = bf16[1,1,2,3072]{3,2,1,0:T(2,128)(2,1)S(1)} all-gather(bf16[1,1,2,768]{3,2,1,0:T(2,128)(2,1)} %param.16), channel_id=1, replica_groups=mesh['cfg'=2,'row'=4,'col'=16] {'row'}, dimensions={3}, use_global_device_ids=true | all-gather | bytes 15360 | tf_op jit(solution)/shard_map/all_gather | solution.py:47
  21.8 10.1 %all_gather.22 = bf16[1,1,2,3072]{3,2,1,0:T(2,128)(2,1)S(1)} all-gather(bf16[1,1,2,768]{3,2,1,0:T(2,128)(2,1)} %param.17), channel_id=1, replica_groups=mesh['cfg'=2,'row'=4,'col'=16] {'row'}, dimensions={3}, use_global_device_ids=true | all-gather | bytes 15360 | tf_op jit(solution)/shard_map/all_gather | solution.py:48
  32.7 19.9 %all-gather.6.cloned.1.call-done = bf16[1,1,512,3072]{3,2,1,0:T(8,128)(2,1)} async-done(((bf16[1,1,512,768]{3,2,1,0:T(8,128)(2,1)}), bf16[1,1,512,3072]{3,2,1,0:T(8,128)(2,1)}) %all-gather.6.cloned.1.call-update) | async-done | bytes 3145744 | tf_op jit(solution)/shard_map/all_gather | solution.py:46
  52.5 2.5 convert_reduce_fusion.1
  55.4 1.0 fusion.15
  56.3 63.7 %all-gather.10.cloned.1.call-done = bf16[1,1,1024,3072]{3,2,1,0:T(8,128)(2,1)} async-done(((bf16[1,1,1024,768]{3,2,1,0:T(8,128)(2,1)}), bf16[1,1,1024,3072]{3,2,1,0:T(8,128)(2,1)}) %all-gather.10.cloned.1.call-update) | async-done | bytes 6291472 | tf_op jit(solution)/shard_map/all_gather | solution.py:45
  120.1 3.8 convert_reduce_fusion
  123.9 0.8 copy-done.1
  124.7 1.8 fusion.8
  126.4 71.7 %all-gather.8.cloned.1.call-done = bf16[3072,2,768]{2,1,0:T(2,128)(2,1)} async-done(((bf16[192,2,768]{2,1,0:T(2,128)(2,1)}), bf16[3072,2,768]{2,1,0:T(2,128)(2,1)}) %all-gather.8.cloned.1.call-update) | async-done | bytes 9437200 | tf_op jit(solution)/shard_map/all_gather | solution.py:58
  198.1 23.8 %copy.27 = bf16[3072,2,768]{0,2,1:T(8,128)(2,1)} copy(bf16[3072,2,768]{2,1,0:T(2,128)(2,1)} %all-gather.8.cloned.1.call-done) | data formatting | bytes 18874368 | tf_op jit(solution)/shard_map/reshape | solution.py:25
  221.9 8.5 %fusion.43 = f32[1,512,2,6,128]{4,1,3,2,0:T(8,128)S(1)} fusion(bf16[2,6,128,3072]{3,2,1,0:T(8,128)(2,1)} %bitcast.111, bf16[1,1,512,3072]{3,2,1,0:T(8,128)(2,1)S(1)} %copy-done.3, f32[3072]{0:T(1024)S(1)} %bitcast.121, f32[3072]{0:T(1024)S(1)} %bitcast.120, f32[512]{0:T(512)S(1)} %add_rsqrt_fusion.4, f32[512]{0:T(512)S(1)} %broadcast_multiply_fusion.1), kind=kOutput, calls=%fused_computation.54 | convolution fusion | flops 4841275392 | bytes 15757312 | tf_op jit(solution)/shard_map/dot_general | solution.py:25
  230.9 1.0 fusion.55
  231.9 1.4 fusion.51
  233.2 64.3 %all-gather.12.cloned.1.call-done = bf16[3072,3,768]{2,0,1:T(8,128)(2,1)} async-done(((bf16[192,3,768]{2,0,1:T(8,128)(2,1)}), bf16[3072,3,768]{2,0,1:T(8,128)(2,1)}) %all-gather.12.cloned.1.call-update) | async-done | bytes 14155792 | tf_op jit(solution)/shard_map/all_gather | solution.py:57
  297.5 18.7 %copy.22 = bf16[3072,3,768]{0,2,1:T(8,128)(2,1)} copy(bf16[3072,3,768]{2,0,1:T(8,128)(2,1)} %all-gather.12.cloned.1.call-done) | data formatting | bytes 28311552 | tf_op jit(solution)/shard_map/all_gather | solution.py:57
  316.3 21.7 %fusion.23 = f32[1,1024,3,6,128]{4,1,3,2,0:T(8,128)S(1)} fusion(bf16[3,6,128,3072]{3,2,1,0:T(8,128)(2,1)} %bitcast.110, bf16[1,1,1024,3072]{3,2,1,0:T(8,128)(2,1)} %all-gather.10.cloned.1.call-done, f32[3072]{0:T(1024)S(1)} %bitcast.119, f32[3072]{0:T(1024)S(1)} %bitcast.118, f32[1024]{0:T(1024)S(1)} %add_rsqrt_fusion.3, f32[1024]{0:T(1024)S(1)} %broadcast_multiply_fusion), kind=kOutput, calls=%fused_computation.31 | convolution fusion | flops 14514388992 | bytes 29917184 | tf_op jit(solution)/shard_map/dot_general | solution.py:25
  337.9 1.7 multiply_reduce_fusion.1
  339.6 1.0 fusion.30
  340.6 0.9 copy-done.2
  341.7 18.4 %fusion = (f32[6,1024]{1,0:T(8,128)S(1)}, f32[6,1024,1536]{2,1,0:T(8,128)}) fusion(pred[1536]{0:T(1024)(128)(4,1)S(1)} %fusion.60, bf16[1024,6,128]{2,0,1:T(8,128)(2,1)S(1)} %fusion.30, bf16[512,6,128]{2,0,1:T(8,128)(2,1)} %fusion.51, f32[1,1024,3,6,128]{4,1,3,2,0:T(8,128)} %copy-done.2, f32[1024,6]{0,1:T(8,128)S(1)} %get-tuple-element.9), kind=kOutput, calls=%fused_computation.2 | convolution fusion | flops 2450515968 | bytes 43304448 | tf_op jit(solution)/shard_map/qhe,khe->hqk/dot_general | solution.py:67
  360.1 15.2 %fusion.46 = bf16[6,128,1024]{2,1,0:T(8,128)(2,1)S(1)} fusion(f32[6,1024,1536]{2,1,0:T(8,128)} %get-tuple-element.7, f32[6,1024]{1,0:T(8,128)S(1)} %get-tuple-element.6, pred[1536]{0:T(1024)(128)(4,1)S(1)} %fusion.60, bf16[1024,6,128]{2,0,1:T(8,128)(2,1)S(1)} %fusion.50, bf16[512,6,128]{2,0,1:T(8,128)(2,1)} %fusion.55), kind=kOutput, calls=%fused_computation.55 | convolution fusion | flops 2459172864 | bytes 41707008 | tf_op jit(solution)/shard_map/hqk,khe->qhe/dot_general | solution.py:73
  375.4 9.4 %convolution_convert_fusion = bf16[1024,3072]{1,0:T(8,128)(2,1)} fusion(bf16[1024,768]{0,1:T(8,128)(2,1)S(1)} %bitcast.122, bf16[768,3072]{0,1:T(8,128)(2,1)} %all-gather.14.cloned.1.call-done), kind=kOutput, calls=%fused_computation.30 | convolution fusion | flops 4834983936 | bytes 12582912 | tf_op jit(solution)/shard_map/dot_general | solution.py:75
  385.7 63.3 %reduce-scatter.6.cloned.1.call-done = bf16[1024,768]{1,0:T(8,128)(2,1)} async-done(((bf16[1024,3072]{1,0:T(8,128)(2,1)}), bf16[1024,768]{1,0:T(8,128)(2,1)}) %reduce-scatter.6.cloned.1.call-update) | async-done | bytes 1572880 | tf_op jit(solution)/shard_map/reduce_scatter | solution.py:81
  449.0 2.9 fusion.54
  454.4 8.0 %reduce-scatter.8.cloned.1.call-done = bf16[1,512,64]{1,2,0:T(8,128)(2,1)} async-done(((bf16[1,1024,64]{1,2,0:T(8,128)(2,1)}), bf16[1,512,64]{1,2,0:T(8,128)(2,1)}) %reduce-scatter.8.cloned.1.call-update) | async-done | bytes 65552 | tf_op jit(solution)/shard_map/reduce_scatter | solution.py:96
  462.4 1.0 copy.28
  464.1 1.6 fusion.57
  465.7 18.5 %reduce-scatter.10.cloned.1.call-done = bf16[128,64]{1,0:T(8,128)(2,1)} async-done(((bf16[512,64]{1,0:T(8,128)(2,1)}), bf16[128,64]{1,0:T(8,128)(2,1)}) %reduce-scatter.10.cloned.1.call-update) | async-done | bytes 16400
  484.2 0.8 reshape_bitcast_fusion
  (49 shorter events, 5.2 us)
Async XLA Ops:
  7.2 441.8 %copy-start = (bf16[768,64]{0,1:T(8,128)(2,1)S(1)}, bf16[768,64]{0,1:T(8,128)(2,1)}, u32[]{:S(2)}) copy-start(bf16[768,64]{0,1:T(8,128)(2,1)} %param.23) | copy-start | bytes 294916
  7.2 45.4 %all-gather.6.cloned.1.call-start = ((), (), s32[]{:S(2)}) async-start(), calls=%async_computation.3 | async-start | bytes 3932160 | tf_op jit(solution)/shard_map/all_gather | solution.py:46
  7.9 112.1 %all-gather.10.cloned.1.call-start = ((), (), s32[]{:S(2)}) async-start(), calls=%async_computation.5 | async-start | bytes 7864320 | tf_op jit(solution)/shard_map/all_gather | solution.py:45
  8.7 189.5 %all-gather.8.cloned.1.call-start = ((), (), s32[]{:S(2)}) async-start(), calls=%async_computation.4 | async-start | bytes 10027008 | tf_op jit(solution)/shard_map/all_gather | solution.py:58
  9.4 288.1 %all-gather.12.cloned.1.call-start = ((), (), s32[]{:S(2)}) async-start(), calls=%async_computation.6 | async-start | bytes 15040512 | tf_op jit(solution)/shard_map/all_gather | solution.py:57
  10.0 365.4 %all-gather.14.cloned.1.call-start = ((), (), s32[]{:S(2)}) async-start(), calls=%async_computation.7 | async-start | bytes 5013504 | tf_op jit(solution)/shard_map/all_gather | solution.py:77
  10.6 438.4 %reduce-scatter.6.cloned.1.call-start = ((), (), s32[]{:S(2)}) async-start(), calls=%async_computation.8 | async-start | bytes 7864320 | tf_op jit(solution)/shard_map/reduce_scatter | solution.py:81
  52.5 2.8 copy-start.3
  120.1 4.6 copy-start.1
  337.9 3.6 copy-start.2
  384.8 0.8 copy-start.7
  384.8 64.2 %copy-start.4 = (bf16[1,1,1024,768]{3,2,1,0:T(8,128)(2,1)S(1)}, bf16[1,1,1024,768]{3,2,1,0:T(8,128)(2,1)}, u32[]{:S(2)}) copy-start(bf16[1,1,1024,768]{3,2,1,0:T(8,128)(2,1)} %param.14) | copy-start | bytes 4718596
  384.8 67.8 %copy-start.8 = (f32[5]{0:T(128)S(1)}, f32[5]{0:T(128)}, u32[]{:S(2)}) copy-start(f32[5]{0:T(128)} %param.25) | copy-start | bytes 64
  384.8 77.6 %reduce-scatter.8.cloned.1.call-start = ((), (), s32[]{:S(2)}) async-start(), calls=%async_computation.9 | async-start | bytes 196608 | tf_op jit(solution)/shard_map/reduce_scatter | solution.py:96
  385.7 99.5 %copy-start.6 = (f32[1,128,64]{1,2,0:T(8,128)S(1)}, f32[1,128,64]{1,2,0:T(8,128)}, u32[]{:S(2)}) copy-start(f32[1,128,64]{1,2,0:T(8,128)} %param.24) | copy-start | bytes 98308
  449.0 15.1 %copy-start.5 = (bf16[1024,768]{1,0:T(8,128)(2,1)S(1)}, bf16[1024,768]{1,0:T(8,128)(2,1)}, u32[]{:S(2)}) copy-start(bf16[1024,768]{1,0:T(8,128)(2,1)} %reduce-scatter.6.cloned.1.call-done) | copy-start | bytes 4718596
  451.9 32.3 %reduce-scatter.10.cloned.1.call-start = ((), (), s32[]{:S(2)}) async-start(), calls=%async_computation.10 | async-start | bytes 163840
Sparse Core Ops, SparseCore 0:
  9.6 42.8 all-gather.5
  54.2 65.8 all-gather.9
  122.2 75.8 all-gather.7
  200.1 97.3 all-gather.11
  299.5 53.3 all-gather.13
  384.9 64.0 reduce-scatter.5
  452.0 10.3 reduce-scatter.7
  464.7 19.4 reduce-scatter.9
where the time goes:
time: 496 us; the launch traced here: 493 us
  waiting for transfers between devices  313 us (63%)
  matrix products  76 us (15%)
  local copies, waits for them, and re-layouts  48.8 us (10%)
  blocking collectives  21.3 us (4%)
  between operations  17.6 us (4%)
  other arithmetic  15.9 us (3%)
    all_gather x1, waiting for transfers between devices, shards(): lax.all_gather(txt_kv_weight, 'col', axis=0, tiled=True)  71.7 us
    all_gather x1, waiting for transfers between devices, shards(): lax.all_gather(img_qkv_weight, 'col', axis=0, tiled=True)  64.3 us
    all_gather x1, waiting for transfers between devices, shards(): lax.all_gather(img_tokens, 'row', axis=3, tiled=True)  63.7 us
    reduce_scatter x1, waiting for transfers between devices, shards(): lax.psum_scatter(head_terms.astype(jnp.bfloat16), 'row', scatter_dimensio...  63.3 us
    dot_general x2, matrix products, add_rows(): jnp.dot(ready, piece.reshape(piece.shape[0], -1), preferred_element_type=...  30.1 us
    reshape x1, local copies, waits for them, and re-layouts, add_rows(): piece.reshape(piece.shape[0], -1)  23.8 us
    unnamed x9, waiting for transfers between devices  21.7 us
    all_gather x1, waiting for transfers between devices, shards(): lax.all_gather(txt_tokens, 'row', axis=3, tiled=True)  19.9 us
  transfers between devices with their start and end apart: 8, of which 7 were waited for; matrix products, arithmetic and copies ran while one was open for 25% of the time, Pallas kernels for 0%

commit v1 on v0

v1 whole, which is shorter than its diff:
```python
import math

import jax
import jax.numpy as jnp
from jax import lax
from jax.sharding import PartitionSpec as P

HD = 128


def rms_norm(values):
    return values * lax.rsqrt(jnp.mean(values * values, -1, keepdims=True) + 1e-06)


def shift_pairs(size, step):
    return [(i, (i + step) % size) for i in range(size)]


def ring_gather(piece, axis_name, size):
    assert size == 4
    from_prev = lax.ppermute(piece, axis_name, shift_pairs(size, 1))
    from_next = lax.ppermute(piece, axis_name, shift_pairs(size, -1))
    cut = piece.shape[0] // 2
    far_top = lax.ppermute(from_prev[:cut], axis_name, shift_pairs(size, 1))
    far_bottom = lax.ppermute(from_next[cut:], axis_name, shift_pairs(size, -1))
    far = jnp.concatenate([far_top, far_bottom], 0)
    return [piece, from_next, far, from_prev]


def modulate_blocks(blocks, mods, width):
    values = [b.astype(jnp.float32) for b in blocks]
    mean = sum(jnp.sum(v, -1, keepdims=True) for v in values) / width
    centred = [v - mean for v in values]
    spread = sum(jnp.sum(c * c, -1, keepdims=True) for c in centred) / width
    scale = lax.rsqrt(spread + 1e-06)
    out = []
    for c, m in zip(centred, mods):
        m = m.astype(jnp.float32)
        out.append(((c * scale) * (1.0 + m[1:2]) + m[0:1]).astype(jnp.bfloat16))
    return jnp.concatenate(out, -1)


def add_rows(piece, ready):
    return jnp.dot(ready, piece.reshape(piece.shape[0], -1), preferred_element_type=jnp.float32)


def shards(
    img_tokens,
    txt_tokens,
    img_mod,
    txt_mod,
    img_gate,
    txt_len,
    img_qkv_weight,
    txt_kv_weight,
    out_weight,
    final_weight,
    latent,
    sigmas,
    step_index,
    guidance,
):
    n_row = 4
    images = img_tokens.shape[2]
    text_slots = txt_tokens.shape[2]
    local_width = img_qkv_weight.shape[2]
    width = local_width * n_row
    heads_here = local_width // HD
    me_row = lax.axis_index("row")
    core = lax.axis_index("cfg")

    bundle = jnp.concatenate(
        [img_tokens[0, 0], img_mod[0, 0], txt_tokens[0, 0], txt_mod[0, 0]], 0
    )
    by_offset = jnp.stack(ring_gather(bundle, "row", n_row))
    blocks = [
        lax.dynamic_index_in_dim(by_offset, (k - me_row) % n_row, 0, keepdims=False)
        for k in range(n_row)
    ]
    txt_base = images + 2
    img_ready = modulate_blocks(
        [b[:images] for b in blocks], [b[images : images + 2] for b in blocks], width
    )
    txt_ready = modulate_blocks(
        [b[txt_base : txt_base + text_slots] for b in blocks],
        [b[txt_base + text_slots : txt_base + text_slots + 2] for b in blocks],
        width,
    )

    img_proj = add_rows(lax.all_gather(img_qkv_weight, "col", axis=0, tiled=True), img_ready)
    txt_proj = add_rows(lax.all_gather(txt_kv_weight, "col", axis=0, tiled=True), txt_ready)
    img_proj = img_proj.reshape(images, 3, heads_here, HD)
    txt_proj = txt_proj.reshape(text_slots, 2, heads_here, HD)
    queries = rms_norm(img_proj[:, 0]).astype(jnp.bfloat16)
    key_rows = jnp.concatenate(
        [rms_norm(txt_proj[:, 0]), rms_norm(img_proj[:, 1])], 0
    ).astype(jnp.bfloat16)
    value_rows = jnp.concatenate([txt_proj[:, 1], img_proj[:, 2]], 0).astype(jnp.bfloat16)
    positions = jnp.arange(text_slots + images, dtype=jnp.int32)
    scores = jnp.einsum(
        "qhe,khe->hqk", queries, key_rows, preferred_element_type=jnp.float32
    ) / math.sqrt(HD)
    usable = (positions < txt_len[0, 0]) | (positions >= text_slots)
    weights = jnp.where(usable, jnp.exp(scores), 0.0)
    chances = (weights / jnp.sum(weights, -1, keepdims=True)).astype(jnp.bfloat16)
    mixed = jnp.einsum("hqk,khe->qhe", chances, value_rows, preferred_element_type=jnp.float32)
    outputs = mixed.reshape(images, local_width).astype(jnp.bfloat16)
    head_terms = jnp.dot(
        outputs,
        lax.all_gather(out_weight, "col", axis=1, tiled=True),
        preferred_element_type=jnp.float32,
    ).astype(jnp.bfloat16)
    term_blocks = head_terms.reshape(images, n_row, local_width)
    projected = lax.dynamic_index_in_dim(term_blocks, me_row, 1, keepdims=False).astype(jnp.float32)
    for step in range(1, n_row):
        outgoing = lax.dynamic_index_in_dim(term_blocks, (me_row + step) % n_row, 1, keepdims=False)
        projected = projected + lax.ppermute(outgoing, "row", shift_pairs(n_row, step)).astype(
            jnp.float32
        )
    gating = img_gate[0].astype(jnp.float32)
    img_out = (img_tokens[0, 0].astype(jnp.float32) + gating * projected).astype(jnp.bfloat16)
    velocity = jnp.dot(img_out, final_weight, preferred_element_type=jnp.float32)
    strength = guidance[0]
    share = jnp.where(core == 1, strength, 1.0 - strength)
    weighted = velocity * share
    n_pair = 2 * n_row
    me_pair = core * n_row + me_row
    rows_each = weighted.shape[0] // n_pair
    velocity_blocks = weighted.reshape(n_pair, rows_each, weighted.shape[1])
    guided = lax.dynamic_index_in_dim(velocity_blocks, me_pair, 0, keepdims=False)
    for step in range(1, n_pair):
        outgoing = lax.dynamic_index_in_dim(velocity_blocks, (me_pair + step) % n_pair, 0, keepdims=False)
        guided = guided + lax.ppermute(outgoing, ("cfg", "row"), shift_pairs(n_pair, step))
    position_now = step_index[0]
    step_size = sigmas[position_now + 1] - sigmas[position_now]
    return (img_out[None, None], latent + step_size * guided[None])


def solution(mesh):
    return jax.shard_map(
        shards,
        mesh=mesh,
        in_specs=(
            P("cfg", "col", None, "row"),
            P("cfg", "col", None, "row"),
            P("cfg", "col", None, "row"),
            P("cfg", "col", None, "row"),
            P("cfg", "col", "row"),
            P("cfg", "col"),
            P("col", None, "row"),
            P("col", None, "row"),
            P("row", "col"),
            P("row", None),
            P("col", ("cfg", "row"), None),
            P(),
            P(),
            P(),
        ),
        out_specs=(P("cfg", "col", None, "row"), P("col", ("cfg", "row"), None)),
        check_vma=False,
    )
```

time: 496 us -> 400 us (0.81)
  waiting for transfers between devices: 313 us -> 167 us
  local copies, waits for them, and re-layouts: 48.8 us -> 83.1 us
  blocking collectives: 21.3 us -> 0 us
  starting transfers between devices: 0.31 us -> 21.5 us
  other arithmetic: 15.9 us -> 32.8 us
    ppermute x0 -> x14, waiting for transfers between devices: none -> 139 us  [the longest x3 63.2 us: shards(): lax.ppermute(outgoing, 'row', shift_pairs(n_row, step)).astype(jnp.float32)]
    all_gather x2 -> x0, waiting for transfers between devices: 83.6 us -> none  [the longest x1 63.7 us: shards(): lax.all_gather(img_tokens, 'row', axis=3, tiled=True)]
    all_gather x1, waiting for transfers between devices: 71.7 us -> 0.01 us  [shards(): lax.all_gather(txt_kv_weight, 'col', axis=0, tiled=True)]
    reduce_scatter x2 -> x0, waiting for transfers between devices: 71.3 us -> none  [the longest x1 63.3 us: shards(): lax.psum_scatter(head_terms.astype(jnp.bfloat16), 'row', scatter_dimensio...]
    all_gather x1, waiting for transfers between devices: 64.3 us -> 26.4 us  [shards(): lax.all_gather(img_qkv_weight, 'col', axis=0, tiled=True)]
    ppermute x0 -> x14, starting transfers between devices: none -> 21.4 us  [the longest x7 9.73 us: shards(): lax.ppermute(outgoing, ('cfg', 'row'), shift_pairs(n_pair, step))]
    all_gather x2 -> x0, blocking collectives: 21.3 us -> none  [the longest x1 11.2 us: shards(): lax.all_gather(img_mod, 'row', axis=3, tiled=True)]
    unnamed x9 -> x3, waiting for transfers between devices: 21.7 us -> 1.39 us
  transfers between devices with their start and end apart: 8 -> 17, of which waited for: 7 -> 8; matrix products, arithmetic and copies ran while one was open for 25% -> 40% of each run, Pallas kernels for 0% -> 0%
where the time goes in v1:
time: 400 us; the launch traced here: 395 us
  waiting for transfers between devices  167 us (42%)
  local copies, waits for them, and re-layouts  83.1 us (21%)
  matrix products  72.8 us (18%)
  other arithmetic  32.8 us (8%)
  starting transfers between devices  21.5 us (5%)
  between operations  18 us (4%)
    ppermute x3, waiting for transfers between devices, shards(): lax.ppermute(outgoing, 'row', shift_pairs(n_row, step)).astype(jnp.float32)  63.2 us
    ppermute x1, waiting for transfers between devices, ring_gather(): from_prev = lax.ppermute(piece, axis_name, shift_pairs(size, 1))  51.2 us
    dot_general x2, matrix products, add_rows(): jnp.dot(ready, piece.reshape(piece.shape[0], -1), preferred_element_type=...  29.2 us
    all_gather x1, waiting for transfers between devices, shards(): lax.all_gather(img_qkv_weight, 'col', axis=0, tiled=True)  26.4 us
    reshape x1, local copies, waits for them, and re-layouts, add_rows(): piece.reshape(piece.shape[0], -1)  23.9 us
    ppermute x1, waiting for transfers between devices, ring_gather(): far_top = lax.ppermute(from_prev[:cut], axis_name, shift_pairs(size, 1))  22.9 us
    all_gather x1, local copies, waits for them, and re-layouts, shards(): lax.all_gather(img_qkv_weight, 'col', axis=0, tiled=True)  18.7 us
    dot_general x1, matrix products, shards(): jnp.einsum('qhe,khe->hqk', queries, key_rows, preferred_element_type=jnp....  18.1 us
  transfers between devices with their start and end apart: 17, of which 8 were waited for; matrix products, arithmetic and copies ran while one was open for 40% of the time, Pallas kernels for 0%

profile of v1, /device:TPU:1, one launch (start us, length us, event | category | flops | bytes accessed | tf_op | source)
XLA Modules:
  0.0 395.2 jit_solution(167567489599963386)
XLA Ops:
  8.7 11.5 %concatenate.20 = bf16[1540,768]{1,0:T(8,128)(2,1)S(1)} concatenate(bf16[1024,768]{1,0:T(8,128)(2,1)} %bitcast.231, bf16[2,768]{1,0:T(2,128)(2,1)} %bitcast.248, bf16[512,768]{1,0:T(8,128)(2,1)} %bitcast.239, bf16[2,768]{1,0:T(2,128)(2,1)} %bitcast.249), dimensions={0} | concatenate | bytes 4730880 | tf_op jit(solution)/shard_map/concatenate | solution.py:72
  20.2 2.5 collective-permute-start.1
  22.7 2.2 collective-permute-start
  24.9 51.2 %collective-permute-done.1 = bf16[1540,768]{1,0:T(8,128)(2,1)S(1)} collective-permute-done((bf16[1540,768]{1,0:T(8,128)(2,1)S(1)}, bf16[1540,768]{1,0:T(8,128)(2,1)S(1)}, u32[]{:S(2)}, u32[]{:S(2)}) %collective-permute-start.1) | collective-permute-done | bytes 2365472 | tf_op jit(solution)/shard_map/ppermute | solution.py:21
  79.8 2.0 collective-permute-start.3
  82.7 22.9 %collective-permute-done.2 = bf16[770,768]{1,0:T(8,128)(2,1)} collective-permute-done((bf16[770,768]{1,0:T(8,128)(2,1)}, bf16[770,768]{1,0:T(8,128)(2,1)}, u32[]{:S(2)}, u32[]{:S(2)}) %collective-permute-start.2) | collective-permute-done | bytes 1182752 | tf_op jit(solution)/shard_map/ppermute | solution.py:24
  106.8 2.0 maximum_bitcast_fusion.4
  108.7 3.4 pad_maximum_fusion
  115.8 2.3 fusion.19
  118.3 3.4 fusion.65
  121.7 4.4 %fusion.15 = (bf16[1024,768]{1,0:T(8,128)(2,1)S(1)}, bf16[1024,768]{1,0:T(8,128)(2,1)S(1)}, bf16[1024,768]{1,0:T(8,128)(2,1)}, bf16[1024,768]{1,0:T(8,128)(2,1)}) fusion(f32[768]{0:T(1024)S(1)} %get-tuple-element.70, f32[768]{0:T(1024)S(1)} %get-tuple-element.71, f32[1024]{0:T(1024)S(1)} %add_rsqrt_fusion.3, f32[1024]{0:T(1024)S(1)} %add_multiply_fusion, ...), kind=kLoop, calls=%fused_computation.28 | loop fusion | flops 18874368 | bytes 12615696 | tf_op jit(solution)/shard_map/convert_element_type | solution.py:39
  126.1 23.9 %copy.37 = bf16[3072,2,768]{0,2,1:T(8,128)(2,1)} copy(bf16[3072,2,768]{2,1,0:T(2,128)(2,1)} %all-gather.4.cloned.1.call-done) | data formatting | bytes 18874368 | tf_op jit(solution)/shard_map/reshape | solution.py:44
  150.0 8.9 %fusion.37 = f32[512,2,6,128]{3,0,2,1:T(8,128)S(1)} fusion(bf16[2,6,128,3072]{3,2,1,0:T(8,128)(2,1)} %bitcast.230, bf16[512,768]{1,0:T(8,128)(2,1)} %get-tuple-element.43, bf16[512,768]{1,0:T(8,128)(2,1)} %get-tuple-element.42, bf16[512,768]{1,0:T(8,128)(2,1)} %get-tuple-element.41, bf16[512,768]{1,0:T(8,128)(2,1)} %get-tuple-element.40), kind=kOutput, calls=%fused_computation.54 | convolution fusion | flops 4844421120 | bytes 15728640 | tf_op jit(solution)/shard_map/dot_general | solution.py:44
  161.8 26.4 %all-gather.6.cloned.1.call-done = bf16[3072,3,768]{2,0,1:T(8,128)(2,1)} async-done(((bf16[192,3,768]{2,0,1:T(8,128)(2,1)}), bf16[3072,3,768]{2,0,1:T(8,128)(2,1)}) %all-gather.6.cloned.1.call-update) | async-done | bytes 14155792 | tf_op jit(solution)/shard_map/all_gather | solution.py:90
  188.2 18.7 %copy.27 = bf16[3072,3,768]{0,2,1:T(8,128)(2,1)} copy(bf16[3072,3,768]{2,0,1:T(8,128)(2,1)} %all-gather.6.cloned.1.call-done) | data formatting | bytes 28311552 | tf_op jit(solution)/shard_map/all_gather | solution.py:90
  206.9 20.3 %fusion.2 = f32[1024,3,6,128]{3,0,2,1:T(8,128)} fusion(bf16[3,6,128,3072]{3,2,1,0:T(8,128)(2,1)} %bitcast.228, bf16[1024,768]{1,0:T(8,128)(2,1)} %get-tuple-element.39, bf16[1024,768]{1,0:T(8,128)(2,1)} %get-tuple-element.38, bf16[1024,768]{1,0:T(8,128)(2,1)S(1)} %get-tuple-element.37, bf16[1024,768]{1,0:T(8,128)(2,1)S(1)} %get-tuple-element.36), kind=kOutput, calls=%fused_computation.6 | convolution fusion | flops 14520680448 | bytes 29884416 | tf_op jit(solution)/shard_map/dot_general | solution.py:44
  227.2 4.6 %multiply_reduce_fusion.1 = (f32[1024,6]{0,1:T(8,128)S(1)}, f32[1024,6]{0,1:T(8,128)S(1)}) fusion(f32[1024,3,6,128]{3,0,2,1:T(8,128)} %fusion.2), kind=kLoop, calls=%fused_computation.70 | loop fusion | flops 3133440 | bytes 6340608 | tf_op jit(solution)/shard_map/reduce_sum | solution.py:12
  231.8 2.4 multiply_convert_fusion
  234.3 2.2 fusion.87
  236.5 18.1 %fusion = (f32[6,1024]{1,0:T(8,128)S(1)}, f32[6,1024,1536]{2,1,0:T(8,128)}) fusion(pred[1536]{0:T(1024)(128)(4,1)S(1)} %fusion.91, bf16[1024,6,128]{2,0,1:T(8,128)(2,1)S(1)} %multiply_convert_fusion, bf16[512,6,128]{2,0,1:T(8,128)(2,1)} %multiply_convert_fusion.3, f32[1024,3,6,128]{3,0,2,1:T(8,128)} %fusion.2, f32[1024,6]{0,1:T(8,128)S(1)} %add_rsqrt_fusion.1), kind=kOutput, calls=%fused_computation.2 | convolution fusion | flops 2450515968 | bytes 43304448 | tf_op jit(solution)/shard_map/qhe,khe->hqk/dot_general | solution.py:100
  254.6 15.5 %fusion.56 = bf16[6,128,1024]{2,1,0:T(8,128)(2,1)S(1)} fusion(f32[6,1024,1536]{2,1,0:T(8,128)} %get-tuple-element.67, f32[6,1024]{1,0:T(8,128)S(1)} %get-tuple-element.66, pred[1536]{0:T(1024)(128)(4,1)S(1)} %fusion.91, bf16[1024,6,128]{2,0,1:T(8,128)(2,1)S(1)} %fusion.87, bf16[512,6,128]{2,0,1:T(8,128)(2,1)} %fusion.90), kind=kOutput, calls=%fused_computation.87 | convolution fusion | flops 2459172864 | bytes 41707008 | tf_op jit(solution)/shard_map/hqk,khe->qhe/dot_general | solution.py:106
  270.1 9.4 %convolution_convert_fusion = bf16[1024,3072]{1,0:T(8,128)(2,1)} fusion(bf16[1024,768]{0,1:T(8,128)(2,1)S(1)} %bitcast.250, bf16[768,3072]{0,1:T(8,128)(2,1)} %all-gather.8.cloned.1.call-done), kind=kOutput, calls=%fused_computation.13 | convolution fusion | flops 4834983936 | bytes 12582912 | tf_op jit(solution)/shard_map/dot_general | solution.py:108
  279.5 8.6 %copy.29 = bf16[1024,3072]{0,1:T(8,128)(2,1)} copy(bf16[1024,3072]{1,0:T(8,128)(2,1)} %convolution_convert_fusion) | data formatting | bytes 12582912 | tf_op jit(solution)/shard_map/convert_element_type | solution.py:112
  288.1 5.2 %constant_dynamic-slice_fusion.15 = (bf16[1024,1,768]{0,2,1:T(8,128)(2,1)S(1)}, bf16[1024,1,768]{0,2,1:T(8,128)(2,1)S(1)}, bf16[1024,1,768]{0,2,1:T(8,128)(2,1)}, bf16[1024,1,768]{0,2,1:T(8,128)(2,1)}) fusion(bf16[1024,4,768]{0,2,1:T(8,128)(2,1)} %bitcast.227, s32[]{:T(128)S(6)} %select_n.133, s32[]{:T(128)S(6)} %select_n.139, s32[]{:T(128)S(6)} %select_n.137, ...), kind=kLoop, calls=%fused_computation.147 | loop fusion | bytes 12582928 | tf_op jit(solution)/shard_map/jit(dynamic_index_in_dim)/dynamic_slice | solution.py:114
  293.4 2.6 copy.31
  297.2 2.6 copy.32
  299.8 2.6 collective-permute-start.5
  306.5 26.1 %collective-permute-done.4 = bf16[1024,768]{1,0:T(8,128)(2,1)} collective-permute-done((bf16[1024,768]{1,0:T(8,128)(2,1)}, bf16[1024,768]{1,0:T(8,128)(2,1)}, u32[]{:S(2)}, u32[]{:S(2)}) %collective-permute-start.4) | collective-permute-done | bytes 1572896 | tf_op jit(solution)/shard_map/ppermute | solution.py:117
  332.5 34.9 %collective-permute-done.5 = bf16[1024,768]{1,0:T(8,128)(2,1)} collective-permute-done((bf16[1024,768]{1,0:T(8,128)(2,1)}, bf16[1024,768]{1,0:T(8,128)(2,1)}, u32[]{:S(2)}, u32[]{:S(2)}) %collective-permute-start.5) | collective-permute-done | bytes 1572896 | tf_op jit(solution)/shard_map/ppermute | solution.py:117
  367.5 2.2 collective-permute-done.6
  369.7 3.9 fusion.48
  376.1 2.2 collective-permute-start.11
  (73 shorter events, 28.2 us)
Async XLA Ops:
  7.2 366.4 %copy-start = (bf16[768,64]{0,1:T(8,128)(2,1)S(1)}, bf16[768,64]{0,1:T(8,128)(2,1)}, u32[]{:S(2)}) copy-start(bf16[768,64]{0,1:T(8,128)(2,1)} %param.23) | copy-start | bytes 294916
  7.2 118.9 %all-gather.4.cloned.1.call-start = ((), (), s32[]{:S(2)}) async-start(), calls=%async_computation | async-start | bytes 10027008 | tf_op jit(solution)/shard_map/all_gather | solution.py:91
  7.9 180.2 %all-gather.6.cloned.1.call-start = ((), (), s32[]{:S(2)}) async-start(), calls=%async_computation.1 | async-start | bytes 15040512 | tf_op jit(solution)/shard_map/all_gather | solution.py:90
  8.7 261.4 %all-gather.8.cloned.1.call-start = ((), (), s32[]{:S(2)}) async-start(), calls=%async_computation.2 | async-start | bytes 5013504 | tf_op jit(solution)/shard_map/all_gather | solution.py:110
  20.2 56.0 %collective-permute-start.1 = (bf16[1540,768]{1,0:T(8,128)(2,1)S(1)}, bf16[1540,768]{1,0:T(8,128)(2,1)S(1)}, u32[]{:S(2)}, u32[]{:S(2)}) collective-permute-start(bf16[1540,768]{1,0:T(8,128)(2,1)S(1)} %concatenate.20), channel_id=1, source_target_pairs={{0,16},{16,32},{32,48},{48,0},{1,17},{17,33},{33,49},{49,1},{2,18}... | collective-permute-start | bytes 7096328 | tf_op jit(solution)/shard_map/ppermute | solution.py:21
  22.7 54.7 %collective-permute-start = (bf16[1540,768]{1,0:T(8,128)(2,1)S(1)}, bf16[1540,768]{1,0:T(8,128)(2,1)S(1)}, u32[]{:S(2)}, u32[]{:S(2)}) collective-permute-start(bf16[1540,768]{1,0:T(8,128)(2,1)S(1)} %concatenate.20), channel_id=1, source_target_pairs={{0,48},{16,0},{32,16},{48,32},{1,49},{17,1},{33,17},{49,33},{2,50}... | collective-permute-start | bytes 7096328 | tf_op jit(solution)/shard_map/ppermute | solution.py:22
  76.1 1.9 copy-start.2
  77.4 28.2 %collective-permute-start.2 = (bf16[770,768]{1,0:T(8,128)(2,1)}, bf16[770,768]{1,0:T(8,128)(2,1)}, u32[]{:S(2)}, u32[]{:S(2)}) collective-permute-start(bf16[770,768]{1,0:T(8,128)(2,1)} %slice.190), channel_id=1, source_target_pairs={{0,16},{16,32},{32,48},{48,0},{1,17},{17,33},{33,49},{49,1},{2,18}... | collective-permute-start | bytes 3548168 | tf_op jit(solution)/shard_map/ppermute | solution.py:24
  78.0 1.8 copy-start.4
  79.8 27.0 %collective-permute-start.3 = (bf16[770,768]{1,0:T(8,128)(2,1)}, bf16[770,768]{1,0:T(8,128)(2,1)}, u32[]{:S(2)}, u32[]{:S(2)}) collective-permute-start(bf16[770,768]{1,0:T(8,128)(2,1)} %slice.191), channel_id=1, source_target_pairs={{0,48},{16,0},{32,16},{48,32},{1,49},{17,1},{33,17},{49,33},{2,50}... | collective-permute-start | bytes 3548168 | tf_op jit(solution)/shard_map/ppermute | solution.py:25
  82.6 26.1 %copy-start.3 = (bf16[1540,768]{1,0:T(8,128)(2,1)S(1)}, bf16[1540,768]{1,0:T(8,128)(2,1)}, u32[]{:S(2)}) copy-start(bf16[1540,768]{1,0:T(8,128)(2,1)} %copy-done.2) | copy-start | bytes 7096324
  82.6 26.1 %copy-start.5 = (bf16[1540,768]{1,0:T(8,128)(2,1)S(1)}, bf16[1540,768]{1,0:T(8,128)(2,1)}, u32[]{:S(2)}) copy-start(bf16[1540,768]{1,0:T(8,128)(2,1)} %copy-done.4) | copy-start | bytes 7096324
  296.0 36.6 %collective-permute-start.4 = (bf16[1024,768]{1,0:T(8,128)(2,1)}, bf16[1024,768]{1,0:T(8,128)(2,1)}, u32[]{:S(2)}, u32[]{:S(2)}) collective-permute-start(bf16[1024,768]{1,0:T(8,128)(2,1)} %bitcast.235), channel_id=1, source_target_pairs={{0,16},{16,32},{32,48},{48,0},{1,17},{17,33},{33,49},{49,1},{2,18}... | collective-permute-start | bytes 4718600 | tf_op jit(solution)/shard_map/ppermute | solution.py:117
  297.2 8.5 %copy-start.7 = (bf16[1,1,768]{2,1,0:T(2,128)(2,1)S(1)}, bf16[1,1,768]{2,1,0:T(2,128)(2,1)}, u32[]{:S(2)}) copy-start(bf16[1,1,768]{2,1,0:T(2,128)(2,1)} %param.18) | copy-start | bytes 4612
  299.8 67.7 %collective-permute-start.5 = (bf16[1024,768]{1,0:T(8,128)(2,1)}, bf16[1024,768]{1,0:T(8,128)(2,1)}, u32[]{:S(2)}, u32[]{:S(2)}) collective-permute-start(bf16[1024,768]{1,0:T(8,128)(2,1)} %bitcast.236), channel_id=1, source_target_pairs={{0,32},{16,48},{32,0},{48,16},{1,33},{17,49},{33,1},{49,17},{2,34}... | collective-permute-start | bytes 4718600 | tf_op jit(solution)/shard_map/ppermute | solution.py:117
  304.0 65.7 %collective-permute-start.6 = (bf16[1024,768]{1,0:T(8,128)(2,1)}, bf16[1024,768]{1,0:T(8,128)(2,1)}, u32[]{:S(2)}, u32[]{:S(2)}) collective-permute-start(bf16[1024,768]{1,0:T(8,128)(2,1)} %bitcast.237), channel_id=1, source_target_pairs={{0,48},{16,0},{32,16},{48,32},{1,49},{17,1},{33,17},{49,33},{2,50}... | collective-permute-start | bytes 4718600 | tf_op jit(solution)/shard_map/ppermute | solution.py:117
  306.5 78.4 %copy-start.8 = (f32[5]{0:T(128)S(1)}, f32[5]{0:T(128)}, u32[]{:S(2)}) copy-start(f32[5]{0:T(128)} %param.25) | copy-start | bytes 64
  306.5 81.1 %copy-start.6 = (f32[1,128,64]{1,2,0:T(8,128)S(1)}, f32[1,128,64]{1,2,0:T(8,128)}, u32[]{:S(2)}) copy-start(f32[1,128,64]{1,2,0:T(8,128)} %param.24) | copy-start | bytes 98308
  373.6 14.7 %copy-start.1 = (bf16[1024,768]{1,0:T(8,128)(2,1)}, bf16[1024,768]{1,0:T(8,128)(2,1)S(1)}, u32[]{:S(2)}) copy-start(bf16[1024,768]{1,0:T(8,128)(2,1)S(1)} %fusion.48) | copy-start | bytes 4718596
  374.4 7.1 %collective-permute-start.10 = (f32[128,64]{0,1:T(8,128)S(1)}, f32[128,64]{0,1:T(8,128)S(1)}, u32[]{:S(2)}, u32[]{:S(2)}) collective-permute-start(f32[128,64]{0,1:T(8,128)S(1)} %bitcast.247), channel_id=1, source_target_pairs={{0,64},{16,80},{32,96},{48,112},{64,0},{80,16},{96,32},{112,48},{1... | collective-permute-start | bytes 98312 | tf_op jit(solution)/shard_map/ppermute | solution.py:133
  376.1 6.6 %collective-permute-start.11 = (f32[128,64]{0,1:T(8,128)S(1)}, f32[128,64]{0,1:T(8,128)S(1)}, u32[]{:S(2)}, u32[]{:S(2)}) collective-permute-start(f32[128,64]{0,1:T(8,128)S(1)} %bitcast.246), channel_id=1, source_target_pairs={{0,80},{16,96},{32,112},{48,0},{64,16},{80,32},{96,48},{112,64},{1... | collective-permute-start | bytes 98312 | tf_op jit(solution)/shard_map/ppermute | solution.py:133
  378.2 8.6 %collective-permute-start.12 = (f32[128,64]{0,1:T(8,128)S(1)}, f32[128,64]{0,1:T(8,128)S(1)}, u32[]{:S(2)}, u32[]{:S(2)}) collective-permute-start(f32[128,64]{0,1:T(8,128)S(1)} %bitcast.245), channel_id=1, source_target_pairs={{0,96},{16,112},{32,0},{48,16},{64,32},{80,48},{96,64},{112,80},{1... | collective-permute-start | bytes 98312 | tf_op jit(solution)/shard_map/ppermute | solution.py:133
  379.9 7.0 %collective-permute-start.13 = (f32[128,64]{0,1:T(8,128)S(1)}, f32[128,64]{0,1:T(8,128)S(1)}, u32[]{:S(2)}, u32[]{:S(2)}) collective-permute-start(f32[128,64]{0,1:T(8,128)S(1)} %bitcast.244), channel_id=1, source_target_pairs={{0,112},{16,0},{32,16},{48,32},{64,48},{80,64},{96,80},{112,96},{1... | collective-permute-start | bytes 98312 | tf_op jit(solution)/shard_map/ppermute | solution.py:133
  381.6 5.3 %collective-permute-start.7 = (f32[128,64]{0,1:T(8,128)S(1)}, f32[128,64]{0,1:T(8,128)S(1)}, u32[]{:S(2)}, u32[]{:S(2)}) collective-permute-start(f32[128,64]{0,1:T(8,128)S(1)} %bitcast.243), channel_id=1, source_target_pairs={{0,16},{16,32},{32,48},{48,64},{64,80},{80,96},{96,112},{112,0},{1... | collective-permute-start | bytes 98312 | tf_op jit(solution)/shard_map/ppermute | solution.py:133
  381.6 5.3 %collective-permute-start.8 = (f32[128,64]{0,1:T(8,128)S(1)}, f32[128,64]{0,1:T(8,128)S(1)}, u32[]{:S(2)}, u32[]{:S(2)}) collective-permute-start(f32[128,64]{0,1:T(8,128)S(1)} %bitcast.242), channel_id=1, source_target_pairs={{0,32},{16,48},{32,64},{48,80},{64,96},{80,112},{96,0},{112,16},{1... | collective-permute-start | bytes 98312 | tf_op jit(solution)/shard_map/ppermute | solution.py:133
  382.7 4.9 %collective-permute-start.9 = (f32[128,64]{0,1:T(8,128)S(1)}, f32[128,64]{0,1:T(8,128)S(1)}, u32[]{:S(2)}, u32[]{:S(2)}) collective-permute-start(f32[128,64]{0,1:T(8,128)S(1)} %bitcast.241), channel_id=1, source_target_pairs={{0,48},{16,64},{32,80},{48,96},{64,112},{80,0},{96,16},{112,32},{1... | collective-permute-start | bytes 98312 | tf_op jit(solution)/shard_map/ppermute | solution.py:133
Sparse Core Ops, SparseCore 0:
  10.1 78.4 all-gather.3
  90.7 97.3 all-gather.5
  190.3 53.3 all-gather.7
